TPU v7x, 128 devices: a whole 4x4x4 slice. The times are simulated.
128 devices in a mesh: req: 8 (over y, core), hid: 16 (over x, z).
Axes of the slice: x: 4, y: 4, z: 4, core: 2. Of those that a mesh axis runs over, the one named last changes fastest.
Arguments:
- tokens: bfloat16 [24576, 1536], P(('req', 'hid')), may hold values from -6 to 6
- segment: int32 [24576], P(('req', 'hid')), may hold values from 0 to 35, as said below
- attn_gain: float32 [1536], replicated, may hold values from 0.1 to 1.9
- w_query: bfloat16 [1536, 1536], replicated, may hold values from -0.2 to 0.2
- w_key: bfloat16 [1536, 512], replicated, may hold values from -0.2 to 0.2
- w_value: bfloat16 [1536, 512], replicated, may hold values from -0.15625 to 0.15625
- q_gain: float32 [64], replicated, may hold values from 0.5 to 6
- k_gain: float32 [64], replicated, may hold values from 0.5 to 6
- w_out: bfloat16 [1536, 1536], replicated, may hold values from -0.15625 to 0.15625
- ffn_gain: float32 [1536], replicated, may hold values from 0.1 to 1.9
- w_gate: bfloat16 [4608, 1536], P(('req', 'hid')), may hold values from -0.15625 to 0.15625
- w_up: bfloat16 [4608, 1536], P(('req', 'hid')), may hold values from -0.15625 to 0.15625
- w_down: bfloat16 [4608, 1536], P(('req', 'hid')), may hold values from -0.09375 to 0.09375
Outputs:
- mixed: bfloat16 [24576, 1536], P(('req', 'hid'))
- kv_cache: bfloat16 [24576, 1024], P(('req', 'hid'))
Inputs may be any that keep to these rules, and one draw needn't show every extreme that they name: Segment ids never fall along the tokens and start at 0. A segment never crosses a boundary between aligned blocks of 3072 tokens; the first block is one segment of exactly 3072 tokens, and every later block holds exactly five segments.
All inputs are finite; a program needn't handle non-finite values.
Results may differ from a plain program's by a relative error of at most 0.015.
Values may be sent and summed in bfloat16 or wider, within the bound.
No kernel may reach another device: no remote copies, remote signals or barrier semaphores. Data moves between devices by JAX's collectives and lax.ppermute only.
A program may use at most 128 MiB of HBM per device.

v0:
```python
import jax
import jax.numpy as jnp
from jax import lax
from jax.sharding import PartitionSpec as P

H = 24
KVH = 8
HD = 64
EPSILON = 1e-05
ROPE_BASE = 1000000.0
NEG_FILL = -1e30
SCORE_SCALE = 0.125


def rms_scale(values, gain):
    mean_sq = jnp.mean(values * values, axis=-1, keepdims=True)
    return values * lax.rsqrt(mean_sq + EPSILON) * gain


def seg_positions(seg_ids):
    indices = jnp.arange(seg_ids.shape[0], dtype=jnp.int32)
    is_first = jnp.concatenate([jnp.ones((1,), bool), seg_ids[1:] != seg_ids[:-1]])
    seg_begin = lax.cummax(jnp.where(is_first, indices, jnp.zeros_like(indices)), axis=0)
    return indices - seg_begin


def rotate(heads, positions):
    half_dim = heads.shape[-1] // 2
    inv_freq = ROPE_BASE ** (-(jnp.arange(half_dim, dtype=jnp.float32) * 2.0) / (2.0 * half_dim))
    angles = positions.astype(jnp.float32)[:, None] * inv_freq[None, :]
    cos_val = jnp.cos(angles)[:, None, :]
    sin_val = jnp.sin(angles)[:, None, :]
    left = heads[..., :half_dim]
    right = heads[..., half_dim:]
    return jnp.concatenate(
        [left * cos_val - right * sin_val, right * cos_val + left * sin_val], axis=-1
    )


def block_length(shard_rows):
    return 4 * shard_rows


def key_block(running, key_blk, val_blk, key_idx, q_grid, seg_start, query_idx):
    run_peak, run_total, run_acc = running
    k_grid = key_blk.reshape(-1, KVH, HD).transpose(1, 0, 2)
    v_grid = val_blk.reshape(-1, KVH, HD).transpose(1, 0, 2)
    scores = (
        jnp.einsum("kgqd,kcd->kgqc", q_grid, k_grid, preferred_element_type=jnp.float32)
        * SCORE_SCALE
    )
    allowed = (key_idx[None, :] <= query_idx[:, None]) & (key_idx[None, :] >= seg_start[:, None])
    scores = jnp.where(allowed, scores, NEG_FILL)
    new_peak = jnp.maximum(run_peak, jnp.max(scores, axis=-1))
    weights = jnp.where(allowed, jnp.exp(scores - new_peak[..., None]), 0.0)
    factor = jnp.exp(run_peak - new_peak)
    new_total = run_total * factor + jnp.sum(weights, axis=-1)
    product = jnp.einsum(
        "kgqc,kcd->kgqd", weights.astype(jnp.bfloat16), v_grid, preferred_element_type=jnp.float32
    )
    return (new_peak, new_total, run_acc * factor[..., None] + product)


def unit_terms(pieces, gathered):
    gate_part, up_part, down_part = pieces
    contract = (((1,), (1,)), ((), ()))
    gate_act = lax.dot_general(gathered, gate_part, contract, preferred_element_type=jnp.float32)
    up_act = lax.dot_general(gathered, up_part, contract, preferred_element_type=jnp.float32)
    hidden = (jax.nn.silu(gate_act) * up_act).astype(jnp.bfloat16)
    return jnp.dot(hidden, down_part, preferred_element_type=jnp.float32)


def gather_by_shifts(part, axis):
    count = lax.psum(1, axis)
    me = lax.axis_index(axis)
    received = [part]
    for shift in range(1, count):
        pairs = [(src, (src + shift) % count) for src in range(count)]
        received.append(lax.ppermute(part, axis, pairs))
    stacked = jnp.stack(received)
    order = (me - jnp.arange(count, dtype=jnp.int32)) % count
    return jnp.take(stacked, order, axis=0).reshape(-1)


def per_device(
    tokens,
    segment,
    attn_gain,
    w_query,
    w_key,
    w_value,
    q_gain,
    k_gain,
    w_out,
    ffn_gain,
    w_gate,
    w_up,
    w_down,
):
    shard_rows = tokens.shape[0]
    groups = H // KVH
    row_base = lax.axis_index("hid") * shard_rows
    group_seg = gather_by_shifts(segment, "hid")
    positions = lax.dynamic_slice_in_dim(seg_positions(group_seg), row_base, shard_rows)
    query_idx = row_base + jnp.arange(shard_rows, dtype=jnp.int32)
    seg_start = query_idx - positions
    resid = tokens.astype(jnp.float32)
    normed = rms_scale(resid, attn_gain).astype(jnp.bfloat16)
    q_raw = jnp.dot(normed, w_query, preferred_element_type=jnp.float32).reshape(shard_rows, H, HD)
    k_raw = jnp.dot(normed, w_key, preferred_element_type=jnp.float32).reshape(shard_rows, KVH, HD)
    queries = rotate(rms_scale(q_raw, q_gain), positions).astype(jnp.bfloat16)
    key_heads = (
        rotate(rms_scale(k_raw, k_gain), positions)
        .astype(jnp.bfloat16)
        .reshape(shard_rows, KVH * HD)
    )
    values = jnp.dot(normed, w_value, preferred_element_type=jnp.float32).astype(jnp.bfloat16)
    kv_cache = jnp.concatenate([key_heads, values], axis=1)
    q_grid = queries.reshape(shard_rows, KVH, groups, HD).transpose(1, 2, 0, 3)
    start_state = (
        jnp.full((KVH, groups, shard_rows), NEG_FILL, jnp.float32),
        jnp.zeros((KVH, groups, shard_rows), jnp.float32),
        jnp.zeros((KVH, groups, shard_rows, HD), jnp.float32),
    )
    kv_part = lax.all_gather(kv_cache, "hid", axis=0, tiled=True)
    unit_rows = lax.all_gather(
        jnp.concatenate([w_gate, w_up, w_down], axis=1), "hid", axis=0, tiled=True
    )
    width = w_gate.shape[1]
    gate_rows = unit_rows[:, :width]
    up_rows = unit_rows[:, width : 2 * width]
    down_rows = unit_rows[:, 2 * width :]
    key_part = kv_part[:, : KVH * HD]
    val_part = kv_part[:, KVH * HD :]
    key_count = key_part.shape[0]
    blk_len = block_length(shard_rows)

    def one_block(block_idx, state_in):
        offset = jnp.asarray(block_idx, jnp.int32) * blk_len
        local_off = jnp.asarray(block_idx, jnp.int32) * blk_len
        key_blk = lax.dynamic_slice_in_dim(key_part, local_off, blk_len)
        val_blk = lax.dynamic_slice_in_dim(val_part, local_off, blk_len)
        key_idx = offset + jnp.arange(blk_len, dtype=jnp.int32)
        return key_block(state_in, key_blk, val_blk, key_idx, q_grid, seg_start, query_idx)

    run_peak, run_total, run_acc = lax.fori_loop(0, key_count // blk_len, one_block, start_state)
    attended = (
        (run_acc / run_total[..., None])
        .transpose(2, 0, 1, 3)
        .reshape(shard_rows, H * HD)
        .astype(jnp.bfloat16)
    )
    after_attn = (resid + jnp.dot(attended, w_out, preferred_element_type=jnp.float32)).astype(
        jnp.bfloat16
    )
    after_f32 = lax.optimization_barrier(after_attn).astype(jnp.float32)
    mlp_in = rms_scale(after_f32, ffn_gain).astype(jnp.bfloat16)
    gathered = lax.all_gather(mlp_in, "req", axis=0, tiled=True)
    unit_sum = unit_terms((gate_rows, up_rows, down_rows), gathered)
    own_share = lax.psum_scatter(
        unit_sum.astype(jnp.bfloat16), "req", scatter_dimension=0, tiled=True
    ).astype(jnp.float32)
    mixed = (after_f32 + own_share).astype(jnp.bfloat16)
    return (mixed, kv_cache)


def solution(mesh):
    placed = (
        P(("req", "hid"), None),
        P(("req", "hid")),
        P(),
        P(),
        P(),
        P(),
        P(),
        P(),
        P(),
        P(),
        P(("req", "hid"), None),
        P(("req", "hid"), None),
        P(("req", "hid"), None),
    )
    return jax.shard_map(
        per_device,
        mesh=mesh,
        in_specs=placed,
        out_specs=(P(("req", "hid"), None), P(("req", "hid"), None)),
        check_vma=False,
    )
```

profile of v0, /device:TPU:0, one launch (start us, length us, event | category | flops | bytes accessed | tf_op | source)
XLA Modules:
  0.0 325.9 jit_solution(5350931809723681569)
XLA Ops:
  7.2 2.1 collective-permute-start
  9.3 6.0 %collective-permute-start.9 = (s32[192]{0:T(256)}, s32[192]{0:T(256)S(1)}, u32[]{:S(2)}, u32[]{:S(2)}) collective-permute-start(s32[192]{0:T(256)} %param.16), channel_id=1, source_target_pairs={{0,10},{1,11},{2,12},{3,13},{4,14},{5,15},{6,0},{7,1},{8,2},{9,3},... | collective-permute-start | bytes 2312 | tf_op jit(solution)/shard_map/ppermute | solution.py:79
  15.4 1.0 collective-permute-start.10
  16.3 1.1 collective-permute-start.11
  17.5 2.0 collective-permute-start.12
  19.5 1.4 fusion.22
  20.9 1.9 multiply_reduce_fusion.1
  23.6 0.6 collective-permute-start.13
  24.2 2.5 collective-permute-start.14
  26.7 2.7 collective-permute-start.1
  29.4 0.9 collective-permute-start.3
  30.3 1.7 collective-permute-start.4
  32.0 3.3 %collective-permute-start.5 = (s32[192]{0:T(256)S(1)}, s32[192]{0:T(256)S(1)}, u32[]{:S(2)}, u32[]{:S(2)}) collective-permute-start(s32[192]{0:T(256)S(1)} %copy-done.7), channel_id=1, source_target_pairs={{0,6},{1,7},{2,8},{3,9},{4,10},{5,11},{6,12},{7,13},{8,14},{9,15},... | collective-permute-start | bytes 2312 | tf_op jit(solution)/shard_map/ppermute | solution.py:79
  35.3 1.9 collective-permute-start.6
  37.2 2.7 collective-permute-start.7
  39.9 1.9 collective-permute-start.8
  42.3 3.3 %collective-permute-done.8 = s32[192]{0:T(256)S(1)} collective-permute-done((s32[192]{0:T(256)S(1)}, s32[192]{0:T(256)S(1)}, u32[]{:S(2)}, u32[]{:S(2)}) %collective-permute-start.8) | collective-permute-done | bytes 800 | tf_op jit(solution)/shard_map/ppermute | solution.py:79
  47.7 0.8 pad_maximum_fusion
  48.6 0.8 maximum_bitcast_fusion.1
  49.7 4.3 %fusion.34 = f32[192,1536]{0,1:T(8,128)S(1)} fusion(bf16[1536,1536]{1,0:T(8,128)(2,1)} %param.18, bf16[192,1536]{1,0:T(8,128)(2,1)S(1)} %copy-done.2, f32[1536]{0:T(1024)S(1)} %copy-done.11, f32[192]{0:T(256)S(1)} %add_rsqrt_fusion.3), kind=kOutput, calls=%fused_computation.87 | convolution fusion | flops 907149312 | bytes 6494976 | tf_op jit(solution)/shard_map/dot_general | solution.py:109
  55.0 56.3 %all-gather.5.cloned.1.call-done = bf16[3072,1024]{1,0:T(8,128)(2,1)} async-done(((bf16[192,1024]{1,0:T(8,128)(2,1)}), bf16[3072,1024]{1,0:T(8,128)(2,1)}) %all-gather.5.cloned.1.call-update) | async-done | bytes 6291472 | tf_op jit(solution)/shard_map/all_gather | solution.py:125
  111.3 5.9 %fusion.39 = (bf16[3072,512]{1,0:T(8,128)(2,1)}, bf16[3072,512]{1,0:T(8,128)(2,1)}) fusion(bf16[3072,1024]{1,0:T(8,128)(2,1)} %all-gather.5.cloned.1.call-done), kind=kLoop, calls=%fused_computation.89 | loop fusion | bytes 12582912 | tf_op jit(solution)/shard_map/slice | solution.py:134
  117.3 98.7 %while.18 = (s32[]{:T(128)}, f32[8,3,192]{2,1,0:T(4,128)S(1)}, f32[8,3,192]{2,1,0:T(4,128)S(1)}, f32[8,3,192,64]{2,3,1,0:T(8,128)}, s32[192]{0:T(256)S(1)}, /*in...) while((s32[]{:T(128)}, f32[8,3,192]{2,1,0:T(4,128)S(1)}, ...), condition=%wide.region_8.9_spmd.clone, body=%wide.region_5.8_spmd.clone.sunk | while | flops 953327040 | bytes 54174144 | solution.py:146
  117.3 1.5 constant_dynamic-slice_fusion.3
  119.2 6.6 %fusion.62 = (f32[8,3,192]{2,1,0:T(4,128)S(1)}, f32[8,768,3,192]{1,3,2,0:T(8,128)}) fusion(pred[192,768]{1,0:T(8,128)(4,1)S(1)} %compare_and_fusion.3, bf16[8,768,64,1]{1,2,3,0:T(8,128)(2,1)S(1)} %bitcast.91, bf16[8,3,192,64]{2,3,1,0:T(8,128)(2,1)S(1)} %get-tuple-element.354), kind=kOutput, calls=%fused_computation.4.clone.1 | convolution fusion | flops 463597056 | bytes 15697920 | tf_op jit(solution)/shard_map/while/body/eval_jaxpr/kgqd,kcd->kgqc/dot_general | solution.py:49
  125.9 7.6 %fusion.63 = f32[8,3,192]{2,1,0:T(4,128)S(1)} fusion(f32[8,768,3,192]{1,3,2,0:T(8,128)} %get-tuple-element.318, f32[8,3,192]{2,1,0:T(4,128)S(1)} %select_maximum_fusion.2, pred[192,768]{1,0:T(8,128)(4,1)S(1)} %compare_and_fusion.3), kind=kLoop, calls=%fused_computation.6.clone.1 | loop fusion | flops 17690112 | bytes 14340096 | tf_op jit(solution)/shard_map/while/body/eval_jaxpr/reduce_sum | solution.py:57
  133.8 8.0 %fusion.65 = f32[8,3,192,64]{2,3,1,0:T(8,128)} fusion(f32[8,3,192,64]{2,3,1,0:T(8,128)} %get-tuple-element.338, bf16[8,768,64,1]{1,2,3,0:T(8,128)(2,1)S(1)} %bitcast.92, f32[8,768,3,192]{1,3,2,0:T(8,128)} %get-tuple-element.318, f32[8,3,192]{2,1,0:T(4,128)S(1)} %select_maximum_fusion.2, pred[192,768]{1,0:T(8,128)(4,1)S(1)} %compare_and_fusion.3, ...), kind=kOutput, calls=%fused_computation.10.clone.1 | convolution fusion | flops 471564288 | bytes 17485824 | tf_op jit(solution)/shard_map/while/body/eval_jaxpr/kgqc,kcd->kgqd/dot_general | solution.py:58
  141.8 1.5 constant_dynamic-slice_fusion.3
  143.8 6.4 %fusion.62 = (f32[8,3,192]{2,1,0:T(4,128)S(1)}, f32[8,768,3,192]{1,3,2,0:T(8,128)}) fusion(pred[192,768]{1,0:T(8,128)(4,1)S(1)} %compare_and_fusion.3, bf16[8,768,64,1]{1,2,3,0:T(8,128)(2,1)S(1)} %bitcast.91, bf16[8,3,192,64]{2,3,1,0:T(8,128)(2,1)S(1)} %get-tuple-element.354), kind=kOutput, calls=%fused_computation.4.clone.1 | convolution fusion | flops 463597056 | bytes 15697920 | tf_op jit(solution)/shard_map/while/body/eval_jaxpr/kgqd,kcd->kgqc/dot_general | solution.py:49
  150.2 7.8 %fusion.63 = f32[8,3,192]{2,1,0:T(4,128)S(1)} fusion(f32[8,768,3,192]{1,3,2,0:T(8,128)} %get-tuple-element.318, f32[8,3,192]{2,1,0:T(4,128)S(1)} %select_maximum_fusion.2, pred[192,768]{1,0:T(8,128)(4,1)S(1)} %compare_and_fusion.3), kind=kLoop, calls=%fused_computation.6.clone.1 | loop fusion | flops 17690112 | bytes 14340096 | tf_op jit(solution)/shard_map/while/body/eval_jaxpr/reduce_sum | solution.py:57
  158.3 8.5 %fusion.65 = f32[8,3,192,64]{2,3,1,0:T(8,128)} fusion(f32[8,3,192,64]{2,3,1,0:T(8,128)} %get-tuple-element.338, bf16[8,768,64,1]{1,2,3,0:T(8,128)(2,1)S(1)} %bitcast.92, f32[8,768,3,192]{1,3,2,0:T(8,128)} %get-tuple-element.318, f32[8,3,192]{2,1,0:T(4,128)S(1)} %select_maximum_fusion.2, pred[192,768]{1,0:T(8,128)(4,1)S(1)} %compare_and_fusion.3, ...), kind=kOutput, calls=%fused_computation.10.clone.1 | convolution fusion | flops 471564288 | bytes 17485824 | tf_op jit(solution)/shard_map/while/body/eval_jaxpr/kgqc,kcd->kgqd/dot_general | solution.py:58
  166.8 1.5 constant_dynamic-slice_fusion.3
  168.8 6.4 %fusion.62 = (f32[8,3,192]{2,1,0:T(4,128)S(1)}, f32[8,768,3,192]{1,3,2,0:T(8,128)}) fusion(pred[192,768]{1,0:T(8,128)(4,1)S(1)} %compare_and_fusion.3, bf16[8,768,64,1]{1,2,3,0:T(8,128)(2,1)S(1)} %bitcast.91, bf16[8,3,192,64]{2,3,1,0:T(8,128)(2,1)S(1)} %get-tuple-element.354), kind=kOutput, calls=%fused_computation.4.clone.1 | convolution fusion | flops 463597056 | bytes 15697920 | tf_op jit(solution)/shard_map/while/body/eval_jaxpr/kgqd,kcd->kgqc/dot_general | solution.py:49
  175.2 7.6 %fusion.63 = f32[8,3,192]{2,1,0:T(4,128)S(1)} fusion(f32[8,768,3,192]{1,3,2,0:T(8,128)} %get-tuple-element.318, f32[8,3,192]{2,1,0:T(4,128)S(1)} %select_maximum_fusion.2, pred[192,768]{1,0:T(8,128)(4,1)S(1)} %compare_and_fusion.3), kind=kLoop, calls=%fused_computation.6.clone.1 | loop fusion | flops 17690112 | bytes 14340096 | tf_op jit(solution)/shard_map/while/body/eval_jaxpr/reduce_sum | solution.py:57
  183.1 8.3 %fusion.65 = f32[8,3,192,64]{2,3,1,0:T(8,128)} fusion(f32[8,3,192,64]{2,3,1,0:T(8,128)} %get-tuple-element.338, bf16[8,768,64,1]{1,2,3,0:T(8,128)(2,1)S(1)} %bitcast.92, f32[8,768,3,192]{1,3,2,0:T(8,128)} %get-tuple-element.318, f32[8,3,192]{2,1,0:T(4,128)S(1)} %select_maximum_fusion.2, pred[192,768]{1,0:T(8,128)(4,1)S(1)} %compare_and_fusion.3, ...), kind=kOutput, calls=%fused_computation.10.clone.1 | convolution fusion | flops 471564288 | bytes 17485824 | tf_op jit(solution)/shard_map/while/body/eval_jaxpr/kgqc,kcd->kgqd/dot_general | solution.py:58
  191.4 1.5 constant_dynamic-slice_fusion.3
  193.4 6.4 %fusion.62 = (f32[8,3,192]{2,1,0:T(4,128)S(1)}, f32[8,768,3,192]{1,3,2,0:T(8,128)}) fusion(pred[192,768]{1,0:T(8,128)(4,1)S(1)} %compare_and_fusion.3, bf16[8,768,64,1]{1,2,3,0:T(8,128)(2,1)S(1)} %bitcast.91, bf16[8,3,192,64]{2,3,1,0:T(8,128)(2,1)S(1)} %get-tuple-element.354), kind=kOutput, calls=%fused_computation.4.clone.1 | convolution fusion | flops 463597056 | bytes 15697920 | tf_op jit(solution)/shard_map/while/body/eval_jaxpr/kgqd,kcd->kgqc/dot_general | solution.py:49
  199.8 7.6 %fusion.63 = f32[8,3,192]{2,1,0:T(4,128)S(1)} fusion(f32[8,768,3,192]{1,3,2,0:T(8,128)} %get-tuple-element.318, f32[8,3,192]{2,1,0:T(4,128)S(1)} %select_maximum_fusion.2, pred[192,768]{1,0:T(8,128)(4,1)S(1)} %compare_and_fusion.3), kind=kLoop, calls=%fused_computation.6.clone.1 | loop fusion | flops 17690112 | bytes 14340096 | tf_op jit(solution)/shard_map/while/body/eval_jaxpr/reduce_sum | solution.py:57
  207.7 8.3 %fusion.65 = f32[8,3,192,64]{2,3,1,0:T(8,128)} fusion(f32[8,3,192,64]{2,3,1,0:T(8,128)} %get-tuple-element.338, bf16[8,768,64,1]{1,2,3,0:T(8,128)(2,1)S(1)} %bitcast.92, f32[8,768,3,192]{1,3,2,0:T(8,128)} %get-tuple-element.318, f32[8,3,192]{2,1,0:T(4,128)S(1)} %select_maximum_fusion.2, pred[192,768]{1,0:T(8,128)(4,1)S(1)} %compare_and_fusion.3, ...), kind=kOutput, calls=%fused_computation.10.clone.1 | convolution fusion | flops 471564288 | bytes 17485824 | tf_op jit(solution)/shard_map/while/body/eval_jaxpr/kgqc,kcd->kgqd/dot_general | solution.py:58
  216.0 1.6 divide_convert_fusion
  217.6 3.6 %fusion.15 = bf16[192,1536]{1,0:T(8,128)(2,1)S(1)} fusion(bf16[192,1536]{0,1:T(8,128)(2,1)S(1)} %bitcast.98, bf16[1536,1536]{1,0:T(8,128)(2,1)} %param.23, bf16[192,1536]{1,0:T(8,128)(2,1)} %param.15), kind=kOutput, calls=%fused_computation.26 | convolution fusion | flops 906854400 | bytes 6488064 | tf_op jit(solution)/shard_map/dot_general | solution.py:153
  221.4 1.0 fusion.27
  222.8 7.7 %reshape.217 = bf16[576,4608]{1,0:T(8,128)(2,1)} reshape(bf16[16,36,4608]{2,1,0:T(8,128)(2,1)} %all-gather.9.cloned.1.call-done) | data formatting | bytes 10616832
  230.5 26.2 %all-gather.7.cloned.1.call-done = bf16[1536,1536]{1,0:T(8,128)(2,1)} async-done(((bf16[192,1536]{1,0:T(8,128)(2,1)}), bf16[1536,1536]{1,0:T(8,128)(2,1)}) %all-gather.7.cloned.1.call-update) | async-done | bytes 4718608 | tf_op jit(solution)/shard_map/all_gather | solution.py:158
  256.7 7.6 %fusion.18 = f32[1536,576]{0,1:T(8,128)} fusion(bf16[1536,1536]{1,0:T(8,128)(2,1)} %all-gather.7.cloned.1.call-done, bf16[576,4608]{1,0:T(8,128)(2,1)} %reshape.217), kind=kOutput, calls=%fused_computation.29 | convolution fusion | flops 2717908992 | bytes 10027008 | tf_op jit(solution)/shard_map/dot_general | solution.py:67
  264.4 13.8 %convolution_convert_fusion = bf16[1536,1536]{1,0:T(8,128)(2,1)} fusion(bf16[576,4608]{1,0:T(8,128)(2,1)} %reshape.217, f32[1536,576]{0,1:T(8,128)} %fusion.18, bf16[1536,1536]{1,0:T(8,128)(2,1)} %all-gather.7.cloned.1.call-done), kind=kOutput, calls=%fused_computation.23 | convolution fusion | flops 5443485696 | bytes 16515072 | tf_op jit(solution)/shard_map/dot_general | solution.py:70
  278.2 39.2 %reduce-scatter.2.cloned.1.call-done = bf16[192,1536]{1,0:T(8,128)(2,1)} async-done(((bf16[1536,1536]{1,0:T(8,128)(2,1)}), bf16[192,1536]{1,0:T(8,128)(2,1)}) %reduce-scatter.2.cloned.1.call-update) | async-done | bytes 589840 | tf_op jit(solution)/shard_map/reduce_scatter | solution.py:160
  317.4 2.0 fusion.28
  (114 shorter events, 8.3 us)
Async XLA Ops:
  7.2 13.7 %copy-start = (bf16[1536,512]{1,0:T(8,128)(2,1)S(1)}, bf16[1536,512]{1,0:T(8,128)(2,1)}, u32[]{:S(2)}) copy-start(bf16[1536,512]{1,0:T(8,128)(2,1)} %param.19) | copy-start | bytes 4718596
  7.2 15.6 %copy-start.2 = (bf16[192,1536]{1,0:T(8,128)(2,1)S(1)}, bf16[192,1536]{1,0:T(8,128)(2,1)}, u32[]{:S(2)}) copy-start(bf16[192,1536]{1,0:T(8,128)(2,1)} %param.15) | copy-start | bytes 1769476
  7.2 15.6 %copy-start.11 = (f32[1536]{0:T(1024)S(1)}, f32[1536]{0:T(1024)}, u32[]{:S(2)}) copy-start(f32[1536]{0:T(1024)} %param.17) | copy-start | bytes 18436
  7.2 104.1 %all-gather.5.cloned.1.call-start = ((), (), s32[]{:S(2)}) async-start(), calls=%async_computation.1 | async-start | bytes 6684672 | tf_op jit(solution)/shard_map/all_gather | solution.py:125
  7.2 16.3 %collective-permute-start = (s32[192]{0:T(256)}, s32[192]{0:T(256)S(1)}, u32[]{:S(2)}, u32[]{:S(2)}) collective-permute-start(s32[192]{0:T(256)} %param.16), channel_id=1, source_target_pairs={{0,1},{1,2},{2,3},{3,4},{4,5},{5,6},{6,7},{7,8},{8,9},{9,10},{10,1... | collective-permute-start | bytes 2312 | tf_op jit(solution)/shard_map/ppermute | solution.py:79
  9.3 14.9 %collective-permute-start.9 = (s32[192]{0:T(256)}, s32[192]{0:T(256)S(1)}, u32[]{:S(2)}, u32[]{:S(2)}) collective-permute-start(s32[192]{0:T(256)} %param.16), channel_id=1, source_target_pairs={{0,10},{1,11},{2,12},{3,13},{4,14},{5,15},{6,0},{7,1},{8,2},{9,3},... | collective-permute-start | bytes 2312 | tf_op jit(solution)/shard_map/ppermute | solution.py:79
  15.4 11.3 %collective-permute-start.10 = (s32[192]{0:T(256)}, s32[192]{0:T(256)S(1)}, u32[]{:S(2)}, u32[]{:S(2)}) collective-permute-start(s32[192]{0:T(256)} %param.16), channel_id=1, source_target_pairs={{0,11},{1,12},{2,13},{3,14},{4,15},{5,0},{6,1},{7,2},{8,3},{9,4},{... | collective-permute-start | bytes 2312 | tf_op jit(solution)/shard_map/ppermute | solution.py:79
  16.3 13.1 %collective-permute-start.11 = (s32[192]{0:T(256)}, s32[192]{0:T(256)S(1)}, u32[]{:S(2)}, u32[]{:S(2)}) collective-permute-start(s32[192]{0:T(256)} %param.16), channel_id=1, source_target_pairs={{0,12},{1,13},{2,14},{3,15},{4,0},{5,1},{6,2},{7,3},{8,4},{9,5},{1... | collective-permute-start | bytes 2312 | tf_op jit(solution)/shard_map/ppermute | solution.py:79
  17.5 11.9 %collective-permute-start.12 = (s32[192]{0:T(256)}, s32[192]{0:T(256)S(1)}, u32[]{:S(2)}, u32[]{:S(2)}) collective-permute-start(s32[192]{0:T(256)} %param.16), channel_id=1, source_target_pairs={{0,13},{1,14},{2,15},{3,0},{4,1},{5,2},{6,3},{7,4},{8,5},{9,6},{10... | collective-permute-start | bytes 2312 | tf_op jit(solution)/shard_map/ppermute | solution.py:79
  19.5 3.3 %copy-start.10 = (bf16[1536,512]{1,0:T(8,128)(2,1)S(1)}, bf16[1536,512]{1,0:T(8,128)(2,1)}, u32[]{:S(2)}) copy-start(bf16[1536,512]{1,0:T(8,128)(2,1)} %param.20) | copy-start | bytes 4718596
  20.9 2.5 copy-start.8
  20.9 2.7 copy-start.7
  22.8 25.8 %copy-start.3 = (bf16[36,1536]{1,0:T(8,128)(2,1)S(1)}, bf16[36,1536]{1,0:T(8,128)(2,1)}, u32[]{:S(2)}) copy-start(bf16[36,1536]{1,0:T(8,128)(2,1)} %param.27) | copy-start | bytes 331780
  22.8 25.8 %copy-start.4 = (bf16[36,1536]{1,0:T(8,128)(2,1)S(1)}, bf16[36,1536]{1,0:T(8,128)(2,1)}, u32[]{:S(2)}) copy-start(bf16[36,1536]{1,0:T(8,128)(2,1)} %param.26) | copy-start | bytes 331780
  22.8 25.8 %copy-start.5 = (bf16[36,1536]{1,0:T(8,128)(2,1)S(1)}, bf16[36,1536]{1,0:T(8,128)(2,1)}, u32[]{:S(2)}) copy-start(bf16[36,1536]{1,0:T(8,128)(2,1)} %param.25) | copy-start | bytes 331780
  23.6 6.7 %collective-permute-start.13 = (s32[192]{0:T(256)S(1)}, s32[192]{0:T(256)S(1)}, u32[]{:S(2)}, u32[]{:S(2)}) collective-permute-start(s32[192]{0:T(256)S(1)} %copy-done.7), channel_id=1, source_target_pairs={{0,14},{1,15},{2,0},{3,1},{4,2},{5,3},{6,4},{7,5},{8,6},{9,7},{10,... | collective-permute-start | bytes 2312 | tf_op jit(solution)/shard_map/ppermute | solution.py:79
  24.2 7.8 %collective-permute-start.14 = (s32[192]{0:T(256)S(1)}, s32[192]{0:T(256)S(1)}, u32[]{:S(2)}, u32[]{:S(2)}) collective-permute-start(s32[192]{0:T(256)S(1)} %copy-done.7), channel_id=1, source_target_pairs={{0,15},{1,0},{2,1},{3,2},{4,3},{5,4},{6,5},{7,6},{8,7},{9,8},{10,9... | collective-permute-start | bytes 2312 | tf_op jit(solution)/shard_map/ppermute | solution.py:79
  26.7 8.7 %collective-permute-start.1 = (s32[192]{0:T(256)S(1)}, s32[192]{0:T(256)S(1)}, u32[]{:S(2)}, u32[]{:S(2)}) collective-permute-start(s32[192]{0:T(256)S(1)} %copy-done.7), channel_id=1, source_target_pairs={{0,2},{1,3},{2,4},{3,5},{4,6},{5,7},{6,8},{7,9},{8,10},{9,11},{10,... | collective-permute-start | bytes 2312 | tf_op jit(solution)/shard_map/ppermute | solution.py:79
  29.4 7.8 %collective-permute-start.2 = (s32[192]{0:T(256)S(1)}, s32[192]{0:T(256)S(1)}, u32[]{:S(2)}, u32[]{:S(2)}) collective-permute-start(s32[192]{0:T(256)S(1)} %copy-done.7), channel_id=1, source_target_pairs={{0,3},{1,4},{2,5},{3,6},{4,7},{5,8},{6,9},{7,10},{8,11},{9,12},{10... | collective-permute-start | bytes 2312 | tf_op jit(solution)/shard_map/ppermute | solution.py:79
  29.4 10.5 %collective-permute-start.3 = (s32[192]{0:T(256)S(1)}, s32[192]{0:T(256)S(1)}, u32[]{:S(2)}, u32[]{:S(2)}) collective-permute-start(s32[192]{0:T(256)S(1)} %copy-done.7), channel_id=1, source_target_pairs={{0,4},{1,5},{2,6},{3,7},{4,8},{5,9},{6,10},{7,11},{8,12},{9,13},{1... | collective-permute-start | bytes 2312 | tf_op jit(solution)/shard_map/ppermute | solution.py:79
  30.3 11.5 %collective-permute-start.4 = (s32[192]{0:T(256)S(1)}, s32[192]{0:T(256)S(1)}, u32[]{:S(2)}, u32[]{:S(2)}) collective-permute-start(s32[192]{0:T(256)S(1)} %copy-done.7), channel_id=1, source_target_pairs={{0,5},{1,6},{2,7},{3,8},{4,9},{5,10},{6,11},{7,12},{8,13},{9,14},{... | collective-permute-start | bytes 2312 | tf_op jit(solution)/shard_map/ppermute | solution.py:79
  32.0 9.8 %collective-permute-start.5 = (s32[192]{0:T(256)S(1)}, s32[192]{0:T(256)S(1)}, u32[]{:S(2)}, u32[]{:S(2)}) collective-permute-start(s32[192]{0:T(256)S(1)} %copy-done.7), channel_id=1, source_target_pairs={{0,6},{1,7},{2,8},{3,9},{4,10},{5,11},{6,12},{7,13},{8,14},{9,15},... | collective-permute-start | bytes 2312 | tf_op jit(solution)/shard_map/ppermute | solution.py:79
  35.3 6.5 %collective-permute-start.6 = (s32[192]{0:T(256)S(1)}, s32[192]{0:T(256)S(1)}, u32[]{:S(2)}, u32[]{:S(2)}) collective-permute-start(s32[192]{0:T(256)S(1)} %copy-done.7), channel_id=1, source_target_pairs={{0,7},{1,8},{2,9},{3,10},{4,11},{5,12},{6,13},{7,14},{8,15},{9,0},... | collective-permute-start | bytes 2312 | tf_op jit(solution)/shard_map/ppermute | solution.py:79
  37.2 5.1 %collective-permute-start.7 = (s32[192]{0:T(256)S(1)}, s32[192]{0:T(256)S(1)}, u32[]{:S(2)}, u32[]{:S(2)}) collective-permute-start(s32[192]{0:T(256)S(1)} %copy-done.7), channel_id=1, source_target_pairs={{0,8},{1,9},{2,10},{3,11},{4,12},{5,13},{6,14},{7,15},{8,0},{9,1},... | collective-permute-start | bytes 2312 | tf_op jit(solution)/shard_map/ppermute | solution.py:79
  39.9 5.7 %collective-permute-start.8 = (s32[192]{0:T(256)S(1)}, s32[192]{0:T(256)S(1)}, u32[]{:S(2)}, u32[]{:S(2)}) collective-permute-start(s32[192]{0:T(256)S(1)} %copy-done.7), channel_id=1, source_target_pairs={{0,9},{1,10},{2,11},{3,12},{4,13},{5,14},{6,15},{7,0},{8,1},{9,2},... | collective-permute-start | bytes 2312 | tf_op jit(solution)/shard_map/ppermute | solution.py:79
  48.5 174.2 %all-gather.9.cloned.1.call-start = ((), (), s32[]{:S(2)}) async-start(), calls=%async_computation.4 | async-start | bytes 6266880 | tf_op jit(solution)/shard_map/all_gather | solution.py:126
  49.4 207.3 %all-gather.7.cloned.1.call-start = ((), (), s32[]{:S(2)}) async-start(), calls=%async_computation.2 | async-start | bytes 5308416 | tf_op jit(solution)/shard_map/all_gather | solution.py:158
  49.7 4.6 %copy-start.9 = (f32[64]{0:T(128)S(1)}, f32[64]{0:T(128)}, u32[]{:S(2)}) copy-start(f32[64]{0:T(128)} %param.21) | copy-start | bytes 772
  217.6 3.8 %copy-start.6 = (f32[1536]{0:T(1024)S(1)}, f32[1536]{0:T(1024)}, u32[]{:S(2)}) copy-start(f32[1536]{0:T(1024)} %param.24) | copy-start | bytes 18436
  222.5 94.9 %reduce-scatter.2.cloned.1.call-start = ((), (), s32[]{:S(2)}) async-start(), calls=%async_computation.3 | async-start | bytes 5308416 | tf_op jit(solution)/shard_map/reduce_scatter | solution.py:160
  278.2 41.2 %copy-start.1 = (bf16[1536,512]{1,0:T(8,128)(2,1)S(1)}, bf16[1536,512]{1,0:T(8,128)(2,1)}, u32[]{:S(2)}) copy-start(bf16[1536,512]{1,0:T(8,128)(2,1)} %param.19) | copy-start | bytes 4718596
Sparse Core Ops, SparseCore 0:
  48.7 62.6 all-gather.4
  113.5 59.1 all-gather.8
  222.6 34.0 all-gather.6
  278.3 39.0 reduce-scatter.1
where the time goes:
time: 327 us; the launch traced here: 326 us
  waiting for transfers between devices  126 us (39%)
  matrix products  90.6 us (28%)
  other arithmetic  41.4 us (13%)
  starting transfers between devices  31 us (9%)
  local copies, waits for them, and re-layouts  22.9 us (7%)
  between operations  14.1 us (4%)
    all_gather x1, waiting for transfers between devices, per_device(): kv_part = lax.all_gather(kv_cache, 'hid', axis=0, tiled=True)  56.3 us
    reduce_scatter x1, waiting for transfers between devices, per_device(): lax.psum_scatter(unit_sum.astype(jnp.bfloat16), 'req', scatter_dimension=...  39.2 us
    dot_general x4, matrix products, key_block(): jnp.einsum('kgqc,kcd->kgqd', weights.astype(jnp.bfloat16), v_grid, prefer...  33 us
    reduce_sum x4, other arithmetic, key_block(): new_total = run_total * factor + jnp.sum(weights, axis=-1)  30.5 us
    ppermute x15, starting transfers between devices, gather_by_shifts(): received.append(lax.ppermute(part, axis, pairs))  30.4 us
    all_gather x1, waiting for transfers between devices, per_device(): gathered = lax.all_gather(mlp_in, 'req', axis=0, tiled=True)  26.2 us
    dot_general x4, matrix products, key_block(): jnp.einsum('kgqd,kcd->kgqc', q_grid, k_grid, preferred_element_type=jnp.f...  25.8 us
    dot_general x1, matrix products, unit_terms(): return jnp.dot(hidden, down_part, preferred_element_type=jnp.float32)  13.8 us
  transfers between devices with their start and end apart: 19, of which 5 were waited for; matrix products, arithmetic and copies ran while one was open for 39% of the time, Pallas kernels for 0%

commit v1 on v0

--- a/solution.py
+++ b/solution.py
@@ -10,6 +10,11 @@
 ROPE_BASE = 1000000.0
 NEG_FILL = -1e30
 SCORE_SCALE = 0.125
+
+
+def gather_over(value, mesh_axis, along):
+    sent = jnp.stack([value] * lax.axis_size(mesh_axis))
+    return jnp.concatenate(lax.all_to_all(sent, mesh_axis, 0, 0), axis=along)
 
 
 def rms_scale(values, gain):
@@ -155,7 +160,7 @@
     )
     after_f32 = lax.optimization_barrier(after_attn).astype(jnp.float32)
     mlp_in = rms_scale(after_f32, ffn_gain).astype(jnp.bfloat16)
-    gathered = lax.all_gather(mlp_in, "req", axis=0, tiled=True)
+    gathered = gather_over(mlp_in, "req", 0)
     unit_sum = unit_terms((gate_rows, up_rows, down_rows), gathered)
     own_share = lax.psum_scatter(
         unit_sum.astype(jnp.bfloat16), "req", scatter_dimension=0, tiled=True

time: 327 us -> 352 us (1.076)
  waiting for transfers between devices: 126 us -> 145 us
  starting transfers between devices: 31 us -> 35.5 us
    all_to_all x0 -> x1, waiting for transfers between devices: none -> 47.3 us  [gather_over(): return jnp.concatenate(lax.all_to_all(sent, mesh_axis, 0, 0), axis=along)]
    all_gather x1 -> x0, waiting for transfers between devices: 26.2 us -> none  [per_device(): gathered = lax.all_gather(mlp_in, 'req', axis=0, tiled=True)]
    all_to_all x0 -> x1, starting transfers between devices: none -> 4.6 us  [gather_over(): return jnp.concatenate(lax.all_to_all(sent, mesh_axis, 0, 0), axis=along)]
  transfers between devices with their start and end apart: 19 -> 19, of which waited for: 5 -> 5; matrix products, arithmetic and copies ran while one was open for 39% -> 37% of each run, Pallas kernels for 0% -> 0%
where the time goes in v1:
time: 352 us; the launch traced here: 351 us
  waiting for transfers between devices  145 us (41%)
  matrix products  90.7 us (26%)
  other arithmetic  40.6 us (12%)
  starting transfers between devices  35.5 us (10%)
  local copies, waits for them, and re-layouts  25.4 us (7%)
  between operations  14.1 us (4%)
    all_gather x1, waiting for transfers between devices, per_device(): kv_part = lax.all_gather(kv_cache, 'hid', axis=0, tiled=True)  56.4 us
    all_to_all x1, waiting for transfers between devices, gather_over(): return jnp.concatenate(lax.all_to_all(sent, mesh_axis, 0, 0), axis=along)  47.3 us
    reduce_scatter x1, waiting for transfers between devices, per_device(): lax.psum_scatter(unit_sum.astype(jnp.bfloat16), 'req', scatter_dimension=...  37.2 us
    dot_general x4, matrix products, key_block(): jnp.einsum('kgqc,kcd->kgqd', weights.astype(jnp.bfloat16), v_grid, prefer...  33.1 us
    reduce_sum x4, other arithmetic, key_block(): new_total = run_total * factor + jnp.sum(weights, axis=-1)  30.5 us
    ppermute x15, starting transfers between devices, gather_by_shifts(): received.append(lax.ppermute(part, axis, pairs))  30.4 us
    dot_general x4, matrix products, key_block(): jnp.einsum('kgqd,kcd->kgqc', q_grid, k_grid, preferred_element_type=jnp.f...  25.8 us
    dot_general x1, matrix products, unit_terms(): return jnp.dot(hidden, down_part, preferred_element_type=jnp.float32)  13.8 us
  transfers between devices with their start and end apart: 19, of which 5 were waited for; matrix products, arithmetic and copies ran while one was open for 37% of the time, Pallas kernels for 0%

profile of v1, /device:TPU:0, one launch (start us, length us, event | category | flops | bytes accessed | tf_op | source)
XLA Modules:
  0.0 351.3 jit_solution(17174085410016462025)
XLA Ops:
  7.2 2.1 collective-permute-start
  9.3 6.0 %collective-permute-start.9 = (s32[192]{0:T(256)}, s32[192]{0:T(256)S(1)}, u32[]{:S(2)}, u32[]{:S(2)}) collective-permute-start(s32[192]{0:T(256)} %param.16), channel_id=1, source_target_pairs={{0,10},{1,11},{2,12},{3,13},{4,14},{5,15},{6,0},{7,1},{8,2},{9,3},... | collective-permute-start | bytes 2312 | tf_op jit(solution)/shard_map/ppermute | solution.py:84
  15.4 1.0 collective-permute-start.10
  16.3 1.1 collective-permute-start.11
  17.5 2.0 collective-permute-start.12
  19.5 1.4 fusion.22
  20.9 1.9 multiply_reduce_fusion.1
  24.2 2.5 collective-permute-start.14
  26.7 2.7 collective-permute-start.1
  29.4 0.9 collective-permute-start.3
  30.3 1.7 collective-permute-start.4
  32.0 3.3 collective-permute-start.5
  35.3 1.9 collective-permute-start.6
  37.2 2.7 collective-permute-start.7
  39.9 1.9 collective-permute-start.8
  42.3 3.3 collective-permute-done.8
  47.7 0.8 pad_maximum_fusion
  48.8 0.8 maximum_bitcast_fusion.1
  49.6 4.3 %fusion.34 = f32[192,1536]{0,1:T(8,128)S(1)} fusion(bf16[1536,1536]{1,0:T(8,128)(2,1)} %param.18, bf16[192,1536]{1,0:T(8,128)(2,1)S(1)} %copy-done.2, f32[1536]{0:T(1024)S(1)} %copy-done.11, f32[192]{0:T(256)S(1)} %add_rsqrt_fusion.3), kind=kOutput, calls=%fused_computation.87 | convolution fusion | flops 907149312 | bytes 6494976 | tf_op jit(solution)/shard_map/dot_general | solution.py:114
  54.9 56.4 %all-gather.4.cloned.1.call-done = bf16[3072,1024]{1,0:T(8,128)(2,1)} async-done(((bf16[192,1024]{1,0:T(8,128)(2,1)}), bf16[3072,1024]{1,0:T(8,128)(2,1)}) %all-gather.4.cloned.1.call-update) | async-done | bytes 6291472 | tf_op jit(solution)/shard_map/all_gather | solution.py:130
  111.3 5.9 %fusion.39 = (bf16[3072,512]{1,0:T(8,128)(2,1)}, bf16[3072,512]{1,0:T(8,128)(2,1)}) fusion(bf16[3072,1024]{1,0:T(8,128)(2,1)} %all-gather.4.cloned.1.call-done), kind=kLoop, calls=%fused_computation.89 | loop fusion | bytes 12582912 | tf_op jit(solution)/shard_map/slice | solution.py:139
  117.3 98.8 %while.18 = (s32[]{:T(128)}, f32[8,3,192]{2,1,0:T(4,128)S(1)}, f32[8,3,192]{2,1,0:T(4,128)S(1)}, f32[8,3,192,64]{2,3,1,0:T(8,128)}, s32[192]{0:T(256)S(1)}, /*in...) while((s32[]{:T(128)}, f32[8,3,192]{2,1,0:T(4,128)S(1)}, ...), condition=%wide.region_8.9_spmd.clone, body=%wide.region_5.8_spmd.clone.sunk | while | flops 953327040 | bytes 54174144 | solution.py:151
  117.3 1.5 constant_dynamic-slice_fusion.3
  119.2 6.6 %fusion.62 = (f32[8,3,192]{2,1,0:T(4,128)S(1)}, f32[8,768,3,192]{1,3,2,0:T(8,128)}) fusion(pred[192,768]{1,0:T(8,128)(4,1)S(1)} %compare_and_fusion.3, bf16[8,768,64,1]{1,2,3,0:T(8,128)(2,1)S(1)} %bitcast.92, bf16[8,3,192,64]{2,3,1,0:T(8,128)(2,1)S(1)} %get-tuple-element.354), kind=kOutput, calls=%fused_computation.4.clone.1 | convolution fusion | flops 463597056 | bytes 15697920 | tf_op jit(solution)/shard_map/while/body/eval_jaxpr/kgqd,kcd->kgqc/dot_general | solution.py:54
  125.9 7.7 %fusion.63 = f32[8,3,192]{2,1,0:T(4,128)S(1)} fusion(f32[8,768,3,192]{1,3,2,0:T(8,128)} %get-tuple-element.318, f32[8,3,192]{2,1,0:T(4,128)S(1)} %select_maximum_fusion.2, pred[192,768]{1,0:T(8,128)(4,1)S(1)} %compare_and_fusion.3), kind=kLoop, calls=%fused_computation.6.clone.1 | loop fusion | flops 17690112 | bytes 14340096 | tf_op jit(solution)/shard_map/while/body/eval_jaxpr/reduce_sum | solution.py:62
  133.9 8.0 %fusion.65 = f32[8,3,192,64]{2,3,1,0:T(8,128)} fusion(f32[8,3,192,64]{2,3,1,0:T(8,128)} %get-tuple-element.338, bf16[8,768,64,1]{1,2,3,0:T(8,128)(2,1)S(1)} %bitcast.93, f32[8,768,3,192]{1,3,2,0:T(8,128)} %get-tuple-element.318, f32[8,3,192]{2,1,0:T(4,128)S(1)} %select_maximum_fusion.2, pred[192,768]{1,0:T(8,128)(4,1)S(1)} %compare_and_fusion.3, ...), kind=kOutput, calls=%fused_computation.10.clone.1 | convolution fusion | flops 471564288 | bytes 17485824 | tf_op jit(solution)/shard_map/while/body/eval_jaxpr/kgqc,kcd->kgqd/dot_general | solution.py:63
  141.9 1.5 constant_dynamic-slice_fusion.3
  143.9 6.4 %fusion.62 = (f32[8,3,192]{2,1,0:T(4,128)S(1)}, f32[8,768,3,192]{1,3,2,0:T(8,128)}) fusion(pred[192,768]{1,0:T(8,128)(4,1)S(1)} %compare_and_fusion.3, bf16[8,768,64,1]{1,2,3,0:T(8,128)(2,1)S(1)} %bitcast.92, bf16[8,3,192,64]{2,3,1,0:T(8,128)(2,1)S(1)} %get-tuple-element.354), kind=kOutput, calls=%fused_computation.4.clone.1 | convolution fusion | flops 463597056 | bytes 15697920 | tf_op jit(solution)/shard_map/while/body/eval_jaxpr/kgqd,kcd->kgqc/dot_general | solution.py:54
  150.3 7.7 %fusion.63 = f32[8,3,192]{2,1,0:T(4,128)S(1)} fusion(f32[8,768,3,192]{1,3,2,0:T(8,128)} %get-tuple-element.318, f32[8,3,192]{2,1,0:T(4,128)S(1)} %select_maximum_fusion.2, pred[192,768]{1,0:T(8,128)(4,1)S(1)} %compare_and_fusion.3), kind=kLoop, calls=%fused_computation.6.clone.1 | loop fusion | flops 17690112 | bytes 14340096 | tf_op jit(solution)/shard_map/while/body/eval_jaxpr/reduce_sum | solution.py:62
  158.3 8.6 %fusion.65 = f32[8,3,192,64]{2,3,1,0:T(8,128)} fusion(f32[8,3,192,64]{2,3,1,0:T(8,128)} %get-tuple-element.338, bf16[8,768,64,1]{1,2,3,0:T(8,128)(2,1)S(1)} %bitcast.93, f32[8,768,3,192]{1,3,2,0:T(8,128)} %get-tuple-element.318, f32[8,3,192]{2,1,0:T(4,128)S(1)} %select_maximum_fusion.2, pred[192,768]{1,0:T(8,128)(4,1)S(1)} %compare_and_fusion.3, ...), kind=kOutput, calls=%fused_computation.10.clone.1 | convolution fusion | flops 471564288 | bytes 17485824 | tf_op jit(solution)/shard_map/while/body/eval_jaxpr/kgqc,kcd->kgqd/dot_general | solution.py:63
  166.9 1.5 constant_dynamic-slice_fusion.3
  168.9 6.4 %fusion.62 = (f32[8,3,192]{2,1,0:T(4,128)S(1)}, f32[8,768,3,192]{1,3,2,0:T(8,128)}) fusion(pred[192,768]{1,0:T(8,128)(4,1)S(1)} %compare_and_fusion.3, bf16[8,768,64,1]{1,2,3,0:T(8,128)(2,1)S(1)} %bitcast.92, bf16[8,3,192,64]{2,3,1,0:T(8,128)(2,1)S(1)} %get-tuple-element.354), kind=kOutput, calls=%fused_computation.4.clone.1 | convolution fusion | flops 463597056 | bytes 15697920 | tf_op jit(solution)/shard_map/while/body/eval_jaxpr/kgqd,kcd->kgqc/dot_general | solution.py:54
  175.3 7.6 %fusion.63 = f32[8,3,192]{2,1,0:T(4,128)S(1)} fusion(f32[8,768,3,192]{1,3,2,0:T(8,128)} %get-tuple-element.318, f32[8,3,192]{2,1,0:T(4,128)S(1)} %select_maximum_fusion.2, pred[192,768]{1,0:T(8,128)(4,1)S(1)} %compare_and_fusion.3), kind=kLoop, calls=%fused_computation.6.clone.1 | loop fusion | flops 17690112 | bytes 14340096 | tf_op jit(solution)/shard_map/while/body/eval_jaxpr/reduce_sum | solution.py:62
  183.2 8.3 %fusion.65 = f32[8,3,192,64]{2,3,1,0:T(8,128)} fusion(f32[8,3,192,64]{2,3,1,0:T(8,128)} %get-tuple-element.338, bf16[8,768,64,1]{1,2,3,0:T(8,128)(2,1)S(1)} %bitcast.93, f32[8,768,3,192]{1,3,2,0:T(8,128)} %get-tuple-element.318, f32[8,3,192]{2,1,0:T(4,128)S(1)} %select_maximum_fusion.2, pred[192,768]{1,0:T(8,128)(4,1)S(1)} %compare_and_fusion.3, ...), kind=kOutput, calls=%fused_computation.10.clone.1 | convolution fusion | flops 471564288 | bytes 17485824 | tf_op jit(solution)/shard_map/while/body/eval_jaxpr/kgqc,kcd->kgqd/dot_general | solution.py:63
  191.5 1.5 constant_dynamic-slice_fusion.3
  193.5 6.4 %fusion.62 = (f32[8,3,192]{2,1,0:T(4,128)S(1)}, f32[8,768,3,192]{1,3,2,0:T(8,128)}) fusion(pred[192,768]{1,0:T(8,128)(4,1)S(1)} %compare_and_fusion.3, bf16[8,768,64,1]{1,2,3,0:T(8,128)(2,1)S(1)} %bitcast.92, bf16[8,3,192,64]{2,3,1,0:T(8,128)(2,1)S(1)} %get-tuple-element.354), kind=kOutput, calls=%fused_computation.4.clone.1 | convolution fusion | flops 463597056 | bytes 15697920 | tf_op jit(solution)/shard_map/while/body/eval_jaxpr/kgqd,kcd->kgqc/dot_general | solution.py:54
  199.9 7.6 %fusion.63 = f32[8,3,192]{2,1,0:T(4,128)S(1)} fusion(f32[8,768,3,192]{1,3,2,0:T(8,128)} %get-tuple-element.318, f32[8,3,192]{2,1,0:T(4,128)S(1)} %select_maximum_fusion.2, pred[192,768]{1,0:T(8,128)(4,1)S(1)} %compare_and_fusion.3), kind=kLoop, calls=%fused_computation.6.clone.1 | loop fusion | flops 17690112 | bytes 14340096 | tf_op jit(solution)/shard_map/while/body/eval_jaxpr/reduce_sum | solution.py:62
  207.8 8.3 %fusion.65 = f32[8,3,192,64]{2,3,1,0:T(8,128)} fusion(f32[8,3,192,64]{2,3,1,0:T(8,128)} %get-tuple-element.338, bf16[8,768,64,1]{1,2,3,0:T(8,128)(2,1)S(1)} %bitcast.93, f32[8,768,3,192]{1,3,2,0:T(8,128)} %get-tuple-element.318, f32[8,3,192]{2,1,0:T(4,128)S(1)} %select_maximum_fusion.2, pred[192,768]{1,0:T(8,128)(4,1)S(1)} %compare_and_fusion.3, ...), kind=kOutput, calls=%fused_computation.10.clone.1 | convolution fusion | flops 471564288 | bytes 17485824 | tf_op jit(solution)/shard_map/while/body/eval_jaxpr/kgqc,kcd->kgqd/dot_general | solution.py:63
  216.1 1.6 divide_convert_fusion
  217.7 3.6 %fusion.15 = bf16[192,1536]{1,0:T(8,128)(2,1)S(1)} fusion(bf16[192,1536]{0,1:T(8,128)(2,1)S(1)} %bitcast.99, bf16[1536,1536]{1,0:T(8,128)(2,1)} %param.23, bf16[192,1536]{1,0:T(8,128)(2,1)} %param.15), kind=kOutput, calls=%fused_computation.26 | convolution fusion | flops 906854400 | bytes 6488064 | tf_op jit(solution)/shard_map/dot_general | solution.py:158
  221.7 2.5 stack.79
  224.2 4.6 %all-to-all-start = ((bf16[8,192,1536]{2,1,0:T(8,128)(2,1)}), bf16[8,192,1536]{2,1,0:T(8,128)(2,1)}, u32[]{:S(2)}, u32[]{:S(2)}) async-start(bf16[8,192,1536]{2,1,0:T(8,128)(2,1)} %stack.79), calls=%async_computation | async-start | bytes 9437184 | tf_op jit(solution)/shard_map/all_to_all | solution.py:17
  229.1 7.7 %reshape.223 = bf16[576,4608]{1,0:T(8,128)(2,1)} reshape(bf16[16,36,4608]{2,1,0:T(8,128)(2,1)} %all-gather.6.cloned.1.call-done) | data formatting | bytes 10616832
  236.8 47.3 %all-to-all-done = bf16[8,192,1536]{2,1,0:T(8,128)(2,1)} async-done(((bf16[8,192,1536]{2,1,0:T(8,128)(2,1)}), bf16[8,192,1536]{2,1,0:T(8,128)(2,1)}, u32[]{:S(2)}, u32[]{:S(2)}) %all-to-all-start) | async-done | bytes 4718624 | tf_op jit(solution)/shard_map/all_to_all | solution.py:17
  284.1 7.6 %fusion.18 = f32[1536,576]{0,1:T(8,128)} fusion(bf16[1536,1536]{1,0:T(8,128)(2,1)} %bitcast.27, bf16[576,4608]{1,0:T(8,128)(2,1)} %reshape.223), kind=kOutput, calls=%fused_computation.29 | convolution fusion | flops 2717908992 | bytes 10027008 | tf_op jit(solution)/shard_map/dot_general | solution.py:72
  291.7 13.8 %convolution_convert_fusion = bf16[1536,1536]{1,0:T(8,128)(2,1)} fusion(bf16[576,4608]{1,0:T(8,128)(2,1)} %reshape.223, f32[1536,576]{0,1:T(8,128)} %fusion.18, bf16[1536,1536]{1,0:T(8,128)(2,1)} %bitcast.27), kind=kOutput, calls=%fused_computation.23 | convolution fusion | flops 5443485696 | bytes 16515072 | tf_op jit(solution)/shard_map/dot_general | solution.py:75
  305.6 37.2 %reduce-scatter.2.cloned.1.call-done = bf16[192,1536]{1,0:T(8,128)(2,1)} async-done(((bf16[1536,1536]{1,0:T(8,128)(2,1)}), bf16[192,1536]{1,0:T(8,128)(2,1)}) %reduce-scatter.2.cloned.1.call-update) | async-done | bytes 589840 | tf_op jit(solution)/shard_map/reduce_scatter | solution.py:165
  342.7 2.0 fusion.28
  (114 shorter events, 9.1 us)
Async XLA Ops:
  7.2 13.7 %copy-start = (bf16[1536,512]{1,0:T(8,128)(2,1)S(1)}, bf16[1536,512]{1,0:T(8,128)(2,1)}, u32[]{:S(2)}) copy-start(bf16[1536,512]{1,0:T(8,128)(2,1)} %param.19) | copy-start | bytes 4718596
  7.2 15.6 %copy-start.2 = (bf16[192,1536]{1,0:T(8,128)(2,1)S(1)}, bf16[192,1536]{1,0:T(8,128)(2,1)}, u32[]{:S(2)}) copy-start(bf16[192,1536]{1,0:T(8,128)(2,1)} %param.15) | copy-start | bytes 1769476
  7.2 15.6 %copy-start.11 = (f32[1536]{0:T(1024)S(1)}, f32[1536]{0:T(1024)}, u32[]{:S(2)}) copy-start(f32[1536]{0:T(1024)} %param.17) | copy-start | bytes 18436
  7.2 104.1 %all-gather.4.cloned.1.call-start = ((), (), s32[]{:S(2)}) async-start(), calls=%async_computation.2 | async-start | bytes 6684672 | tf_op jit(solution)/shard_map/all_gather | solution.py:130
  7.2 16.3 %collective-permute-start = (s32[192]{0:T(256)}, s32[192]{0:T(256)S(1)}, u32[]{:S(2)}, u32[]{:S(2)}) collective-permute-start(s32[192]{0:T(256)} %param.16), channel_id=1, source_target_pairs={{0,1},{1,2},{2,3},{3,4},{4,5},{5,6},{6,7},{7,8},{8,9},{9,10},{10,1... | collective-permute-start | bytes 2312 | tf_op jit(solution)/shard_map/ppermute | solution.py:84
  9.3 14.9 %collective-permute-start.9 = (s32[192]{0:T(256)}, s32[192]{0:T(256)S(1)}, u32[]{:S(2)}, u32[]{:S(2)}) collective-permute-start(s32[192]{0:T(256)} %param.16), channel_id=1, source_target_pairs={{0,10},{1,11},{2,12},{3,13},{4,14},{5,15},{6,0},{7,1},{8,2},{9,3},... | collective-permute-start | bytes 2312 | tf_op jit(solution)/shard_map/ppermute | solution.py:84
  15.4 11.3 %collective-permute-start.10 = (s32[192]{0:T(256)}, s32[192]{0:T(256)S(1)}, u32[]{:S(2)}, u32[]{:S(2)}) collective-permute-start(s32[192]{0:T(256)} %param.16), channel_id=1, source_target_pairs={{0,11},{1,12},{2,13},{3,14},{4,15},{5,0},{6,1},{7,2},{8,3},{9,4},{... | collective-permute-start | bytes 2312 | tf_op jit(solution)/shard_map/ppermute | solution.py:84
  16.3 13.1 %collective-permute-start.11 = (s32[192]{0:T(256)}, s32[192]{0:T(256)S(1)}, u32[]{:S(2)}, u32[]{:S(2)}) collective-permute-start(s32[192]{0:T(256)} %param.16), channel_id=1, source_target_pairs={{0,12},{1,13},{2,14},{3,15},{4,0},{5,1},{6,2},{7,3},{8,4},{9,5},{1... | collective-permute-start | bytes 2312 | tf_op jit(solution)/shard_map/ppermute | solution.py:84
  17.5 11.9 %collective-permute-start.12 = (s32[192]{0:T(256)}, s32[192]{0:T(256)S(1)}, u32[]{:S(2)}, u32[]{:S(2)}) collective-permute-start(s32[192]{0:T(256)} %param.16), channel_id=1, source_target_pairs={{0,13},{1,14},{2,15},{3,0},{4,1},{5,2},{6,3},{7,4},{8,5},{9,6},{10... | collective-permute-start | bytes 2312 | tf_op jit(solution)/shard_map/ppermute | solution.py:84
  19.5 3.3 copy-start.10
  20.9 2.5 copy-start.8
  20.9 2.7 copy-start.7
  22.8 26.0 %copy-start.3 = (bf16[36,1536]{1,0:T(8,128)(2,1)S(1)}, bf16[36,1536]{1,0:T(8,128)(2,1)}, u32[]{:S(2)}) copy-start(bf16[36,1536]{1,0:T(8,128)(2,1)} %param.27) | copy-start | bytes 331780
  22.8 25.9 %copy-start.4 = (bf16[36,1536]{1,0:T(8,128)(2,1)S(1)}, bf16[36,1536]{1,0:T(8,128)(2,1)}, u32[]{:S(2)}) copy-start(bf16[36,1536]{1,0:T(8,128)(2,1)} %param.26) | copy-start | bytes 331780
  22.8 25.9 %copy-start.5 = (bf16[36,1536]{1,0:T(8,128)(2,1)S(1)}, bf16[36,1536]{1,0:T(8,128)(2,1)}, u32[]{:S(2)}) copy-start(bf16[36,1536]{1,0:T(8,128)(2,1)} %param.25) | copy-start | bytes 331780
  23.6 6.7 %collective-permute-start.13 = (s32[192]{0:T(256)S(1)}, s32[192]{0:T(256)S(1)}, u32[]{:S(2)}, u32[]{:S(2)}) collective-permute-start(s32[192]{0:T(256)S(1)} %copy-done.7), channel_id=1, source_target_pairs={{0,14},{1,15},{2,0},{3,1},{4,2},{5,3},{6,4},{7,5},{8,6},{9,7},{10,... | collective-permute-start | bytes 2312 | tf_op jit(solution)/shard_map/ppermute | solution.py:84
  24.2 7.8 %collective-permute-start.14 = (s32[192]{0:T(256)S(1)}, s32[192]{0:T(256)S(1)}, u32[]{:S(2)}, u32[]{:S(2)}) collective-permute-start(s32[192]{0:T(256)S(1)} %copy-done.7), channel_id=1, source_target_pairs={{0,15},{1,0},{2,1},{3,2},{4,3},{5,4},{6,5},{7,6},{8,7},{9,8},{10,9... | collective-permute-start | bytes 2312 | tf_op jit(solution)/shard_map/ppermute | solution.py:84
  26.7 8.7 %collective-permute-start.1 = (s32[192]{0:T(256)S(1)}, s32[192]{0:T(256)S(1)}, u32[]{:S(2)}, u32[]{:S(2)}) collective-permute-start(s32[192]{0:T(256)S(1)} %copy-done.7), channel_id=1, source_target_pairs={{0,2},{1,3},{2,4},{3,5},{4,6},{5,7},{6,8},{7,9},{8,10},{9,11},{10,... | collective-permute-start | bytes 2312 | tf_op jit(solution)/shard_map/ppermute | solution.py:84
  29.4 7.8 %collective-permute-start.2 = (s32[192]{0:T(256)S(1)}, s32[192]{0:T(256)S(1)}, u32[]{:S(2)}, u32[]{:S(2)}) collective-permute-start(s32[192]{0:T(256)S(1)} %copy-done.7), channel_id=1, source_target_pairs={{0,3},{1,4},{2,5},{3,6},{4,7},{5,8},{6,9},{7,10},{8,11},{9,12},{10... | collective-permute-start | bytes 2312 | tf_op jit(solution)/shard_map/ppermute | solution.py:84
  29.4 10.5 %collective-permute-start.3 = (s32[192]{0:T(256)S(1)}, s32[192]{0:T(256)S(1)}, u32[]{:S(2)}, u32[]{:S(2)}) collective-permute-start(s32[192]{0:T(256)S(1)} %copy-done.7), channel_id=1, source_target_pairs={{0,4},{1,5},{2,6},{3,7},{4,8},{5,9},{6,10},{7,11},{8,12},{9,13},{1... | collective-permute-start | bytes 2312 | tf_op jit(solution)/shard_map/ppermute | solution.py:84
  30.3 11.5 %collective-permute-start.4 = (s32[192]{0:T(256)S(1)}, s32[192]{0:T(256)S(1)}, u32[]{:S(2)}, u32[]{:S(2)}) collective-permute-start(s32[192]{0:T(256)S(1)} %copy-done.7), channel_id=1, source_target_pairs={{0,5},{1,6},{2,7},{3,8},{4,9},{5,10},{6,11},{7,12},{8,13},{9,14},{... | collective-permute-start | bytes 2312 | tf_op jit(solution)/shard_map/ppermute | solution.py:84
  32.0 9.8 %collective-permute-start.5 = (s32[192]{0:T(256)S(1)}, s32[192]{0:T(256)S(1)}, u32[]{:S(2)}, u32[]{:S(2)}) collective-permute-start(s32[192]{0:T(256)S(1)} %copy-done.7), channel_id=1, source_target_pairs={{0,6},{1,7},{2,8},{3,9},{4,10},{5,11},{6,12},{7,13},{8,14},{9,15},... | collective-permute-start | bytes 2312 | tf_op jit(solution)/shard_map/ppermute | solution.py:84
  35.3 6.5 %collective-permute-start.6 = (s32[192]{0:T(256)S(1)}, s32[192]{0:T(256)S(1)}, u32[]{:S(2)}, u32[]{:S(2)}) collective-permute-start(s32[192]{0:T(256)S(1)} %copy-done.7), channel_id=1, source_target_pairs={{0,7},{1,8},{2,9},{3,10},{4,11},{5,12},{6,13},{7,14},{8,15},{9,0},... | collective-permute-start | bytes 2312 | tf_op jit(solution)/shard_map/ppermute | solution.py:84
  37.2 5.1 %collective-permute-start.7 = (s32[192]{0:T(256)S(1)}, s32[192]{0:T(256)S(1)}, u32[]{:S(2)}, u32[]{:S(2)}) collective-permute-start(s32[192]{0:T(256)S(1)} %copy-done.7), channel_id=1, source_target_pairs={{0,8},{1,9},{2,10},{3,11},{4,12},{5,13},{6,14},{7,15},{8,0},{9,1},... | collective-permute-start | bytes 2312 | tf_op jit(solution)/shard_map/ppermute | solution.py:84
  39.9 5.7 %collective-permute-start.8 = (s32[192]{0:T(256)S(1)}, s32[192]{0:T(256)S(1)}, u32[]{:S(2)}, u32[]{:S(2)}) collective-permute-start(s32[192]{0:T(256)S(1)} %copy-done.7), channel_id=1, source_target_pairs={{0,9},{1,10},{2,11},{3,12},{4,13},{5,14},{6,15},{7,0},{8,1},{9,2},... | collective-permute-start | bytes 2312 | tf_op jit(solution)/shard_map/ppermute | solution.py:84
  48.5 180.6 %all-gather.6.cloned.1.call-start = ((), (), s32[]{:S(2)}) async-start(), calls=%async_computation.4 | async-start | bytes 6266880 | tf_op jit(solution)/shard_map/all_gather | solution.py:131
  49.6 4.6 %copy-start.9 = (f32[64]{0:T(128)S(1)}, f32[64]{0:T(128)}, u32[]{:S(2)}) copy-start(f32[64]{0:T(128)} %param.21) | copy-start | bytes 772
  217.7 3.8 %copy-start.6 = (f32[1536]{0:T(1024)S(1)}, f32[1536]{0:T(1024)}, u32[]{:S(2)}) copy-start(f32[1536]{0:T(1024)} %param.24) | copy-start | bytes 18436
  224.2 59.9 %all-to-all-start = ((bf16[8,192,1536]{2,1,0:T(8,128)(2,1)}), bf16[8,192,1536]{2,1,0:T(8,128)(2,1)}, u32[]{:S(2)}, u32[]{:S(2)}) async-start(bf16[8,192,1536]{2,1,0:T(8,128)(2,1)} %stack.79), calls=%async_computation | async-start | bytes 9437184 | tf_op jit(solution)/shard_map/all_to_all | solution.py:17
  228.8 113.9 %reduce-scatter.2.cloned.1.call-start = ((), (), s32[]{:S(2)}) async-start(), calls=%async_computation.3 | async-start | bytes 5308416 | tf_op jit(solution)/shard_map/reduce_scatter | solution.py:165
  305.5 39.2 %copy-start.1 = (bf16[1536,512]{1,0:T(8,128)(2,1)S(1)}, bf16[1536,512]{1,0:T(8,128)(2,1)}, u32[]{:S(2)}) copy-start(bf16[1536,512]{1,0:T(8,128)(2,1)} %param.19) | copy-start | bytes 4718596
Sparse Core Ops, SparseCore 0:
  48.7 62.6 all-gather.3
  114.1 59.1 all-gather.5
  305.7 36.9 reduce-scatter.1
